TPU v7x, 256 devices: a whole 4x4x8 slice. The times are simulated.
256 devices in a mesh: lat: 16 (over y_lo, z), lon: 16 (over y_hi, x, core).
Axes of the slice: x: 4, y: 4 (y_hi: 2, y_lo: 2; y = y_hi * 2 + y_lo), z: 8, core: 2. Of those that a mesh axis runs over, the one named last changes fastest.
Arguments:
- prognostic: float32 [6, 2, 2304, 2048], P(None, None, 'lon', 'lat'), may hold values from -6 to 6
- wind_zonal: float32 [2, 2048], P(None, 'lat'), may hold values from -1 to 1
- wind_merid: float32 [2, 2048], P(None, 'lat'), may hold values from -0.5 to 0.5
- layer_depth: float32 [2], replicated, may hold values from 0.25 to 1
- diffusion: float32 [3, 2], replicated, may hold values from 0.05 to 0.4
Outputs:
- prognostic_out: float32 [6, 2, 2304, 2048], P(None, None, 'lon', 'lat')
All inputs are finite; a program needn't handle non-finite values.
Results may differ from a plain program's by a relative error of at most 0.00013.
Values sent between devices are 32-bit elements; how exact they have to be, the bound alone decides.
No kernel may reach another device: no remote copies, remote signals or barrier semaphores. Data moves between devices by JAX's collectives and lax.ppermute only.
A program may use at most 128 MiB of HBM per device.

v0:
```python
import math
import jax
import jax.numpy as jnp
from jax import lax
from jax.sharding import PartitionSpec as P

ITERS = 3
time_step = 0.15
highest = lax.Precision.HIGHEST


def with_halo(block, sides, width, periodic):
    for axis, dim in sides:
        count = lax.axis_size(axis)
        forward = [(i, i + 1) for i in range(count - 1)]
        if periodic:
            forward.append((count - 1, 0))
        backward = [(target, source) for source, target in forward]
        low = lax.ppermute(
            lax.slice_in_dim(block, block.shape[dim] - width, None, axis=dim), axis, forward
        )
        high = lax.ppermute(lax.slice_in_dim(block, 0, width, axis=dim), axis, backward)
        block = jnp.concatenate([low, block, high], axis=dim)
    return block


def latitude(row_ids, lat_total):
    return (row_ids.astype(jnp.float32) + 0.5) * (math.pi / lat_total) - 0.5 * math.pi


def damping(row_ids, lat_total, circle_len):
    cos_ratio = jnp.cos(latitude(row_ids, lat_total)) / math.cos(0.25 * math.pi)
    wave_ids = jnp.arange(circle_len // 2 + 1)
    sine_vals = jnp.sin(wave_ids.astype(jnp.float32) * (math.pi / circle_len))
    safe_sines = jnp.where(wave_ids == 0, 1.0, sine_vals)
    return jnp.where(
        wave_ids[None, :] == 0, 1.0, jnp.minimum(1.0, cos_ratio[:, None] / safe_sines[None, :])
    )


def tendency(
    fields_now,
    north_rows,
    south_rows,
    east_cols,
    west_cols,
    row_ids,
    lat_total,
    wind_zonal,
    wind_merid,
    layer_depth,
    diffusion,
):
    latitudes = latitude(row_ids, lat_total)
    cos_centre = jnp.cos(latitudes)
    cos_north = jnp.cos(latitude(row_ids + 1, lat_total))
    cos_south = jnp.cos(latitude(row_ids - 1, lat_total))
    coriolis = jnp.sin(latitudes)
    zonal_diff = (east_cols - west_cols) / (2.0 * cos_centre)
    merid_diff = 0.5 * (north_rows - south_rows)
    advect = wind_zonal[:, None, :] * zonal_diff + wind_merid[:, None, :] * merid_diff
    diverge = zonal_diff[0] + (north_rows[1] * cos_north - south_rows[1] * cos_south) / (
        2.0 * cos_centre
    )
    zonal_tend = -advect[0] + coriolis * fields_now[1] - zonal_diff[2]
    merid_tend = -advect[1] - coriolis * fields_now[0] - merid_diff[2]
    height_tend = -advect[2] - layer_depth[:, None, None] * diverge
    tracer_tend = -advect[3:] + diffusion[:, :, None, None] * (
        north_rows[3:] - 2.0 * fields_now[3:] + south_rows[3:]
    )
    return jnp.concatenate(
        [zonal_tend[None], merid_tend[None], height_tend[None], tracer_tend], axis=0
    )


def split_length(total):
    first = int(math.isqrt(total))
    while total % first != 0:
        first = first - 1
    return (first, total // first)


def trig_table(length):
    counts = jnp.arange(length, dtype=jnp.int32)
    phases = counts[:, None] * counts[None, :] % length
    angles = phases.astype(jnp.float32) * (2.0 * math.pi / length)
    return (jnp.cos(angles), jnp.sin(angles))


def twist_table(outer, inner, total):
    outer_ids = jnp.arange(outer, dtype=jnp.int32)
    inner_ids = jnp.arange(inner, dtype=jnp.int32)
    angles = (outer_ids[:, None] * inner_ids[None, :] % total).astype(jnp.float32) * (
        2.0 * math.pi / total
    )
    return (jnp.cos(angles)[None], jnp.sin(angles)[None])


def forward_real(signal):
    vectors, total = signal.shape
    inner, outer = split_length(total)
    grid = signal.reshape(vectors, outer, inner)
    cos_outer, sin_outer = trig_table(outer)
    first_re = jnp.einsum("mba,bk->mka", grid, cos_outer, precision=highest)
    first_im = -jnp.einsum("mba,bk->mka", grid, sin_outer, precision=highest)
    twist_cos, twist_sin = twist_table(outer, inner, total)
    mid_re = first_re * twist_cos + first_im * twist_sin
    mid_im = first_im * twist_cos - first_re * twist_sin
    cos_inner, sin_inner = trig_table(inner)
    last_re = jnp.einsum("mka,aq->mqk", mid_re, cos_inner, precision=highest) + jnp.einsum(
        "mka,aq->mqk", mid_im, sin_inner, precision=highest
    )
    last_im = jnp.einsum("mka,aq->mqk", mid_im, cos_inner, precision=highest) - jnp.einsum(
        "mka,aq->mqk", mid_re, sin_inner, precision=highest
    )
    return (last_re.reshape(vectors, total), last_im.reshape(vectors, total))


def inverse_real(spec_re, spec_im):
    vectors, total = spec_re.shape
    inner, outer = split_length(total)
    grid_re = spec_re.reshape(vectors, outer, inner)
    grid_im = spec_im.reshape(vectors, outer, inner)
    cos_outer, sin_outer = trig_table(outer)
    first_re = jnp.einsum("mba,bk->mka", grid_re, cos_outer, precision=highest) - jnp.einsum(
        "mba,bk->mka", grid_im, sin_outer, precision=highest
    )
    first_im = jnp.einsum("mba,bk->mka", grid_im, cos_outer, precision=highest) + jnp.einsum(
        "mba,bk->mka", grid_re, sin_outer, precision=highest
    )
    twist_cos, twist_sin = twist_table(outer, inner, total)
    mid_re = first_re * twist_cos - first_im * twist_sin
    mid_im = first_im * twist_cos + first_re * twist_sin
    cos_inner, sin_inner = trig_table(inner)
    last_re = jnp.einsum("mka,aq->mqk", mid_re, cos_inner, precision=highest) - jnp.einsum(
        "mka,aq->mqk", mid_im, sin_inner, precision=highest
    )
    return last_re.reshape(vectors, total)


def local(prognostic, wind_zonal, wind_merid, layer_depth, diffusion):
    field_count, level_count, col_count, row_count = prognostic.shape
    lat_devs = lax.axis_size("lat")
    lon_devs = lax.axis_size("lon")
    lat_total = row_count * lat_devs
    circle_len = col_count * lon_devs
    lat_pos = lax.axis_index("lat")
    lon_pos = lax.axis_index("lon")
    row_ids = lat_pos * row_count + jnp.arange(row_count, dtype=jnp.int32)
    quarter = lat_devs // 4
    is_polar = (lat_pos < quarter) | (lat_pos >= lat_devs - quarter)

    def smooth(sector, start_row):
        vectors, total, slab_rows = sector.shape
        halfway = damping(start_row + jnp.arange(slab_rows, dtype=jnp.int32), lat_total, circle_len)
        mirrored = halfway[:, 1 : circle_len // 2][:, ::-1]
        factors = jnp.concatenate([halfway, mirrored], axis=1)[None]
        rows_last = jnp.transpose(sector, (0, 2, 1)).reshape(vectors * slab_rows, total)
        spec_re, spec_im = forward_real(rows_last)
        spec_re = (spec_re.reshape(vectors, slab_rows, total) * factors).reshape(
            vectors * slab_rows, total
        )
        spec_im = (spec_im.reshape(vectors, slab_rows, total) * factors).reshape(
            vectors * slab_rows, total
        )
        back = inverse_real(spec_re, spec_im) * (1.0 / circle_len)
        return jnp.transpose(back.reshape(vectors, slab_rows, total), (0, 2, 1))

    fields_now = prognostic
    for substep in range(ITERS):
        lat_padded = with_halo(fields_now, (("lat", 3),), 1, False)
        lon_padded = with_halo(fields_now, (("lon", 2),), 1, True)
        tendency_now = tendency(
            fields_now,
            lat_padded[:, :, :, 2:],
            lat_padded[:, :, :, :-2],
            lon_padded[:, :, 2:],
            lon_padded[:, :, :-2],
            row_ids,
            lat_total,
            wind_zonal,
            wind_merid,
            layer_depth,
            diffusion,
        )
        flattened = tendency_now.reshape(field_count * level_count, col_count, row_count)

        def filter_sector(sector):
            slab_rows = sector.shape[2]
            start_row = lat_pos * row_count + lon_pos * slab_rows
            damped = lax.cond(
                is_polar, lambda inner: smooth(inner, start_row), lambda inner: inner, sector
            )
            return lax.all_to_all(damped, "lon", split_axis=1, concat_axis=2, tiled=True)

        filtered = filter_sector(
            lax.all_to_all(flattened, "lon", split_axis=2, concat_axis=1, tiled=True)
        )
        fields_now = fields_now + time_step * filtered.reshape(fields_now.shape)
    return fields_now


def solution(mesh):
    return jax.shard_map(
        local,
        mesh=mesh,
        in_specs=(P(None, None, "lon", "lat"), P(None, "lat"), P(None, "lat"), P(), P()),
        out_specs=P(None, None, "lon", "lat"),
        check_vma=False,
    )
```

profile of v0, /device:TPU:96, one launch (start us, length us, event | category | flops | bytes accessed | tf_op | source)
XLA Modules:
  0.0 506.7 jit_solution(1772880354401610135)
XLA Ops:
  1.0 5.3 %collective-permute-start = (f32[6,2,1,128]{3,1,2,0:T(2,128)S(1)}, f32[6,2,1,128]{3,1,2,0:T(2,128)S(1)}, u32[]{:S(2)}, u32[]{:S(2)}) collective-permute-start(f32[6,2,1,128]{3,1,2,0:T(2,128)S(1)} %bitcast.258), channel_id=1, source_target_pairs={{1,0},{2,1},{3,2},{4,3},{5,4},{6,5},{7,6},{8,7},{9,8},{10,9},{11,1... | collective-permute-start | bytes 18440 | tf_op jit(solution)/shard_map/ppermute | solution.py:22
  10.0 5.0 collective-permute-start.3
  23.9 3.9 reshape.286
  27.8 5.0 all-to-all-start
  32.9 16.2 %all-to-all-done = f32[16,1,13824]{2,1,0:T(1,128)S(1)} async-done(((f32[16,1,13824]{2,1,0:T(1,128)}), f32[16,1,13824]{2,1,0:T(1,128)S(1)}, u32[]{:S(2)}, u32[]{:S(2)}) %all-to-all-start) | async-done | bytes 884768 | tf_op jit(solution)/shard_map/all_to_all | solution.py:197
  63.1 36.6 %conditional.3 = (f32[12,2304,8]{1,2,0:T(8,128)S(1)}) conditional(s32[]{:T(128)} %convert_element_type.240, f32[12,2304,8]{1,2,0:T(8,128)S(1)} %all_to_all.72, (f32[12,2304,8]{1,2,0:T(8,128)S(1)}, s32[]{:T(128)}) %tuple.23), branch_computations={%region_0.0_spmd, %region_1.2_spmd} | conditional | flops 1533790208 | bytes 46552336 | solution.py:191
  99.8 5.4 %copy.262 = f32[12,2304,8]{0,2,1:T(8,128)} copy(f32[12,2304,8]{1,2,0:T(8,128)S(1)} %get-tuple-element.85) | data formatting | bytes 1769472 | tf_op jit(solution)/shard_map/cond | solution.py:191
  105.2 10.5 %reshape.288 = f32[16,1,13824]{2,1,0:T(1,128)S(1)} reshape(f32[2304,8,12]{2,1,0:T(8,128)} %bitcast.230) | data formatting | bytes 1769472
  115.7 19.3 %all_to_all.90 = f32[16,1,13824]{2,1,0:T(1,128)} all-to-all(f32[16,1,13824]{2,1,0:T(1,128)S(1)} %reshape.288), channel_id=1, replica_groups=mesh['lat'=16,'lon'=16] {'lon'}, dimensions={0} | all-to-all | bytes 1769472 | tf_op jit(solution)/shard_map/all_to_all | solution.py:194
  138.9 14.7 %reshape.289 = f32[2304,8,12]{2,1,0:T(8,128)} reshape(f32[16,13824]{1,0:T(8,128)S(1)} %reduce.1) | data formatting | bytes 1769472
  153.6 8.5 %broadcast_multiply_fusion.2 = f32[12,2304,8]{0,2,1:T(8,128)} fusion(f32[2304,8,12]{2,1,0:T(8,128)} %reshape.289), kind=kLoop, calls=%fused_computation.377 | loop fusion | flops 221184 | bytes 1769472 | tf_op jit(solution)/shard_map/mul | solution.py:199
  162.0 8.1 %copy.263 = f32[12,16,144,8]{2,3,1,0:T(8,128)} copy(f32[12,16,144,8]{0,3,2,1:T(8,128)} %bitcast.231) | data formatting | bytes 1769472 | tf_op jit(solution)/shard_map/mul | solution.py:199
  173.7 5.1 %collective-permute-start.7 = (f32[6,2,144,1]{2,3,1,0:T(1,128)S(1)}, f32[6,2,144,1]{2,3,1,0:T(1,128)S(1)}, u32[]{:S(2)}, u32[]{:S(2)}) collective-permute-start(f32[6,2,144,1]{2,3,1,0:T(1,128)S(1)} %get-tuple-element.78), channel_id=1, source_target_pairs={{0,16},{16,32},{32,48},{48,64},{64,80},{80,96},{96,112},{112,128},... | collective-permute-start | bytes 20744 | tf_op jit(solution)/shard_map/ppermute | solution.py:19
  182.2 4.6 collective-permute-done.5
  197.0 20.3 %all_to_all.91 = f32[16,1,13824]{2,1,0:T(1,128)} all-to-all(f32[16,1,13824]{2,1,0:T(1,128)S(1)} %reshape.290), channel_id=1, replica_groups=mesh['lat'=16,'lon'=16] {'lon'}, dimensions={0} | all-to-all | bytes 1769472 | tf_op jit(solution)/shard_map/all_to_all | solution.py:197
  229.6 36.6 %conditional.4 = (f32[12,2304,8]{1,2,0:T(8,128)S(1)}) conditional(s32[]{:T(128)} %convert_element_type.240, f32[12,2304,8]{1,2,0:T(8,128)S(1)} %all_to_all.77, (f32[12,2304,8]{1,2,0:T(8,128)S(1)}, s32[]{:T(128)}) %tuple.24), branch_computations={%region_2.3_spmd, %region_3.4_spmd} | conditional | flops 1533790208 | bytes 46552336 | solution.py:191
  266.3 5.4 %copy.272 = f32[12,2304,8]{0,2,1:T(8,128)} copy(f32[12,2304,8]{1,2,0:T(8,128)S(1)} %get-tuple-element.86) | data formatting | bytes 1769472 | tf_op jit(solution)/shard_map/cond | solution.py:191
  271.7 10.5 %reshape.292 = f32[16,1,13824]{2,1,0:T(1,128)S(1)} reshape(f32[2304,8,12]{2,1,0:T(8,128)} %bitcast.232) | data formatting | bytes 1769472
  282.2 19.3 %all_to_all.92 = f32[16,1,13824]{2,1,0:T(1,128)} all-to-all(f32[16,1,13824]{2,1,0:T(1,128)S(1)} %reshape.292), channel_id=1, replica_groups=mesh['lat'=16,'lon'=16] {'lon'}, dimensions={0} | all-to-all | bytes 1769472 | tf_op jit(solution)/shard_map/all_to_all | solution.py:194
  305.4 14.7 %reshape.293 = f32[2304,8,12]{2,1,0:T(8,128)} reshape(f32[16,13824]{1,0:T(8,128)S(1)} %reduce.3) | data formatting | bytes 1769472
  320.1 8.5 %broadcast_multiply_fusion.1 = f32[12,2304,8]{0,2,1:T(8,128)} fusion(f32[2304,8,12]{2,1,0:T(8,128)} %reshape.293), kind=kLoop, calls=%fused_computation.376 | loop fusion | flops 221184 | bytes 1769472 | tf_op jit(solution)/shard_map/mul | solution.py:199
  328.6 8.1 %copy.273 = f32[12,16,144,8]{2,3,1,0:T(8,128)} copy(f32[12,16,144,8]{0,3,2,1:T(8,128)} %bitcast.233) | data formatting | bytes 1769472 | tf_op jit(solution)/shard_map/mul | solution.py:199
  340.2 5.1 %collective-permute-start.11 = (f32[6,2,144,1]{2,3,1,0:T(1,128)S(1)}, f32[6,2,144,1]{2,3,1,0:T(1,128)S(1)}, u32[]{:S(2)}, u32[]{:S(2)}) collective-permute-start(f32[6,2,144,1]{2,3,1,0:T(1,128)S(1)} %get-tuple-element.74), channel_id=1, source_target_pairs={{0,16},{16,32},{32,48},{48,64},{64,80},{80,96},{96,112},{112,128},... | collective-permute-start | bytes 20744 | tf_op jit(solution)/shard_map/ppermute | solution.py:19
  348.8 4.8 collective-permute-done.9
  363.8 20.3 %all_to_all.93 = f32[16,1,13824]{2,1,0:T(1,128)} all-to-all(f32[16,1,13824]{2,1,0:T(1,128)S(1)} %reshape.294), channel_id=1, replica_groups=mesh['lat'=16,'lon'=16] {'lon'}, dimensions={0} | all-to-all | bytes 1769472 | tf_op jit(solution)/shard_map/all_to_all | solution.py:197
  396.4 36.5 %conditional.5 = (f32[12,2304,8]{1,2,0:T(8,128)S(1)}) conditional(s32[]{:T(128)} %convert_element_type.240, f32[12,2304,8]{1,2,0:T(8,128)S(1)} %all_to_all.82, (f32[12,2304,8]{1,2,0:T(8,128)S(1)}, s32[]{:T(128)}) %tuple.25), branch_computations={%region_4.5_spmd, %region_5.6_spmd} | conditional | flops 1533790208 | bytes 46552336 | solution.py:191
  432.9 5.4 %copy.281 = f32[12,2304,8]{0,2,1:T(8,128)} copy(f32[12,2304,8]{1,2,0:T(8,128)S(1)} %get-tuple-element.87) | data formatting | bytes 1769472 | tf_op jit(solution)/shard_map/cond | solution.py:191
  438.3 10.5 %reshape.296 = f32[16,1,13824]{2,1,0:T(1,128)S(1)} reshape(f32[2304,8,12]{2,1,0:T(8,128)} %bitcast.234) | data formatting | bytes 1769472
  448.9 19.3 %all_to_all.94 = f32[16,1,13824]{2,1,0:T(1,128)} all-to-all(f32[16,1,13824]{2,1,0:T(1,128)S(1)} %reshape.296), channel_id=1, replica_groups=mesh['lat'=16,'lon'=16] {'lon'}, dimensions={0} | all-to-all | bytes 1769472 | tf_op jit(solution)/shard_map/all_to_all | solution.py:194
  472.0 14.7 %reshape.297 = f32[2304,8,12]{2,1,0:T(8,128)} reshape(f32[16,13824]{1,0:T(8,128)S(1)} %reduce.5) | data formatting | bytes 1769472
  486.7 8.5 %broadcast_multiply_fusion = f32[12,2304,8]{0,2,1:T(8,128)} fusion(f32[2304,8,12]{2,1,0:T(8,128)} %reshape.297), kind=kLoop, calls=%fused_computation.375 | loop fusion | flops 221184 | bytes 1769472 | tf_op jit(solution)/shard_map/mul | solution.py:199
  495.2 8.1 %copy.282 = f32[12,16,144,8]{2,3,1,0:T(8,128)} copy(f32[12,16,144,8]{0,3,2,1:T(8,128)} %bitcast.235) | data formatting | bytes 1769472 | tf_op jit(solution)/shard_map/mul | solution.py:199
  (175 shorter events, 208.9 us)
Async XLA Ops:
  0.8 15.7 %collective-permute-start.1 = (f32[6,2,1,128]{3,1,2,0:T(2,128)S(1)}, f32[6,2,1,128]{3,1,2,0:T(2,128)S(1)}, u32[]{:S(2)}, u32[]{:S(2)}) collective-permute-start(f32[6,2,1,128]{3,1,2,0:T(2,128)S(1)} %bitcast.257), channel_id=1, source_target_pairs={{0,1},{1,2},{2,3},{3,4},{4,5},{5,6},{6,7},{7,8},{8,9},{9,10},{10,1... | collective-permute-start | bytes 18440 | tf_op jit(solution)/shard_map/ppermute | solution.py:19
  0.9 14.2 %copy-start.6 = (f32[2,128]{1,0:T(2,128)S(1)}, f32[2,128]{1,0:T(2,128)}, u32[]{:S(2)}) copy-start(f32[2,128]{1,0:T(2,128)} %param.13) | copy-start | bytes 3076
  0.9 14.3 %copy-start.5 = (f32[3,2]{0,1:T(2,128)S(1)}, f32[3,2]{0,1:T(2,128)}, u32[]{:S(2)}) copy-start(f32[3,2]{0,1:T(2,128)} %param.15) | copy-start | bytes 76
  1.0 14.4 %collective-permute-start = (f32[6,2,1,128]{3,1,2,0:T(2,128)S(1)}, f32[6,2,1,128]{3,1,2,0:T(2,128)S(1)}, u32[]{:S(2)}, u32[]{:S(2)}) collective-permute-start(f32[6,2,1,128]{3,1,2,0:T(2,128)S(1)} %bitcast.258), channel_id=1, source_target_pairs={{1,0},{2,1},{3,2},{4,3},{5,4},{6,5},{7,6},{8,7},{9,8},{10,9},{11,1... | collective-permute-start | bytes 18440 | tf_op jit(solution)/shard_map/ppermute | solution.py:22
  7.9 9.8 %copy-start.3 = (f32[2,128]{1,0:T(2,128)S(1)}, f32[2,128]{1,0:T(2,128)}, u32[]{:S(2)}) copy-start(f32[2,128]{1,0:T(2,128)} %param.12) | copy-start | bytes 3076
  8.0 9.8 %collective-permute-start.2 = (f32[6,2,144,1]{2,3,1,0:T(1,128)S(1)}, f32[6,2,144,1]{2,3,1,0:T(1,128)S(1)}, u32[]{:S(2)}, u32[]{:S(2)}) collective-permute-start(f32[6,2,144,1]{2,3,1,0:T(1,128)S(1)} %get-tuple-element.79), channel_id=1, source_target_pairs={{16,0},{32,16},{48,32},{64,48},{80,64},{96,80},{112,96},{128,112},... | collective-permute-start | bytes 20744 | tf_op jit(solution)/shard_map/ppermute | solution.py:22
  10.0 7.7 %collective-permute-start.3 = (f32[6,2,144,1]{2,3,1,0:T(1,128)S(1)}, f32[6,2,144,1]{2,3,1,0:T(1,128)S(1)}, u32[]{:S(2)}, u32[]{:S(2)}) collective-permute-start(f32[6,2,144,1]{2,3,1,0:T(1,128)S(1)} %get-tuple-element.80), channel_id=1, source_target_pairs={{0,16},{16,32},{32,48},{48,64},{64,80},{80,96},{96,112},{112,128},... | collective-permute-start | bytes 20744 | tf_op jit(solution)/shard_map/ppermute | solution.py:19
  20.6 0.7 copy-start.4
  27.8 21.3 %all-to-all-start = ((f32[16,1,13824]{2,1,0:T(1,128)}), f32[16,1,13824]{2,1,0:T(1,128)S(1)}, u32[]{:S(2)}, u32[]{:S(2)}) async-start(f32[16,1,13824]{2,1,0:T(1,128)} %reshape.286), calls=%async_computation | async-start | bytes 1769472 | tf_op jit(solution)/shard_map/all_to_all | solution.py:197
  79.8 1.5 copy-start
  171.8 16.2 %collective-permute-start.6 = (f32[6,2,144,1]{2,3,1,0:T(1,128)S(1)}, f32[6,2,144,1]{2,3,1,0:T(1,128)S(1)}, u32[]{:S(2)}, u32[]{:S(2)}) collective-permute-start(f32[6,2,144,1]{2,3,1,0:T(1,128)S(1)} %get-tuple-element.77), channel_id=1, source_target_pairs={{16,0},{32,16},{48,32},{64,48},{80,64},{96,80},{112,96},{128,112},... | collective-permute-start | bytes 20744 | tf_op jit(solution)/shard_map/ppermute | solution.py:22
  173.7 14.3 %collective-permute-start.7 = (f32[6,2,144,1]{2,3,1,0:T(1,128)S(1)}, f32[6,2,144,1]{2,3,1,0:T(1,128)S(1)}, u32[]{:S(2)}, u32[]{:S(2)}) collective-permute-start(f32[6,2,144,1]{2,3,1,0:T(1,128)S(1)} %get-tuple-element.78), channel_id=1, source_target_pairs={{0,16},{16,32},{32,48},{48,64},{64,80},{80,96},{96,112},{112,128},... | collective-permute-start | bytes 20744 | tf_op jit(solution)/shard_map/ppermute | solution.py:19
  179.4 1.6 collective-permute-start.4
  180.0 6.9 %collective-permute-start.5 = (f32[6,2,1,128]{3,1,2,0:T(2,128)S(1)}, f32[6,2,1,128]{3,1,2,0:T(2,128)S(1)}, u32[]{:S(2)}, u32[]{:S(2)}) collective-permute-start(f32[6,2,1,128]{3,1,2,0:T(2,128)S(1)} %copy.267), channel_id=1, source_target_pairs={{0,1},{1,2},{2,3},{3,4},{4,5},{5,6},{6,7},{7,8},{8,9},{9,10},{10,1... | collective-permute-start | bytes 18440 | tf_op jit(solution)/shard_map/ppermute | solution.py:19
  246.4 1.5 copy-start.1
  338.3 16.5 %collective-permute-start.10 = (f32[6,2,144,1]{2,3,1,0:T(1,128)S(1)}, f32[6,2,144,1]{2,3,1,0:T(1,128)S(1)}, u32[]{:S(2)}, u32[]{:S(2)}) collective-permute-start(f32[6,2,144,1]{2,3,1,0:T(1,128)S(1)} %get-tuple-element.73), channel_id=1, source_target_pairs={{16,0},{32,16},{48,32},{64,48},{80,64},{96,80},{112,96},{128,112},... | collective-permute-start | bytes 20744 | tf_op jit(solution)/shard_map/ppermute | solution.py:22
  340.2 14.6 %collective-permute-start.11 = (f32[6,2,144,1]{2,3,1,0:T(1,128)S(1)}, f32[6,2,144,1]{2,3,1,0:T(1,128)S(1)}, u32[]{:S(2)}, u32[]{:S(2)}) collective-permute-start(f32[6,2,144,1]{2,3,1,0:T(1,128)S(1)} %get-tuple-element.74), channel_id=1, source_target_pairs={{0,16},{16,32},{32,48},{48,64},{64,80},{80,96},{96,112},{112,128},... | collective-permute-start | bytes 20744 | tf_op jit(solution)/shard_map/ppermute | solution.py:19
  345.9 1.6 collective-permute-start.8
  346.5 7.1 %collective-permute-start.9 = (f32[6,2,1,128]{3,1,2,0:T(2,128)S(1)}, f32[6,2,1,128]{3,1,2,0:T(2,128)S(1)}, u32[]{:S(2)}, u32[]{:S(2)}) collective-permute-start(f32[6,2,1,128]{3,1,2,0:T(2,128)S(1)} %copy.276), channel_id=1, source_target_pairs={{0,1},{1,2},{2,3},{3,4},{4,5},{5,6},{6,7},{7,8},{8,9},{9,10},{10,1... | collective-permute-start | bytes 18440 | tf_op jit(solution)/shard_map/ppermute | solution.py:19
  413.1 1.5 copy-start.2
where the time goes:
time: 514 us; the launch traced here: 507 us
  local copies, waits for them, and re-layouts  226 us (44%)
  blocking collectives  98.4 us (19%)
  other arithmetic  65.3 us (13%)
  matrix products  54.4 us (11%)
  starting transfers between devices  33.4 us (6%)
  waiting for transfers between devices  26.6 us (5%)
    unnamed x22, local copies, waits for them, and re-layouts  96.9 us
    all_to_all x3, blocking collectives, filter_sector(): lax.all_to_all(damped, 'lon', split_axis=1, concat_axis=2, tiled=True)  57.8 us
    all_to_all x2, blocking collectives, local(): lax.all_to_all(flattened, 'lon', split_axis=2, concat_axis=1, tiled=True)  40.6 us
    mul x3, other arithmetic, local(): fields_now = fields_now + time_step * filtered.reshape(fields_now.shape)  25.4 us
    mul x3, local copies, waits for them, and re-layouts, local(): fields_now = fields_now + time_step * filtered.reshape(fields_now.shape)  24.3 us
    mul x9, local copies, waits for them, and re-layouts, smooth(): spec_re.reshape(vectors, slab_rows, total) * factors  22 us
    all_to_all x7, local copies, waits for them, and re-layouts, local(): lax.all_to_all(flattened, 'lon', split_axis=2, concat_axis=1, tiled=True)  18.3 us
    ppermute x6, starting transfers between devices, with_halo(): lax.ppermute(lax.slice_in_dim(block, block.shape[dim] - width, None, axis...  16.6 us
  transfers between devices with their start and end apart: 13, of which 5 were waited for; matrix products, arithmetic and copies ran while one was open for 2% of the time, Pallas kernels for 0%

commit v1 on v0

--- a/solution.py
+++ b/solution.py
@@ -7,6 +7,13 @@
 ITERS = 3
 time_step = 0.15
 highest = lax.Precision.HIGHEST
+
+
+def trade_parts(value, axis, split, join):
+    n_dev = lax.axis_size(axis)
+    pieces = jnp.stack(jnp.split(value, n_dev, axis=split), axis=0)
+    pieces = lax.all_to_all(pieces, axis, split_axis=0, concat_axis=0)
+    return jnp.concatenate(pieces, axis=join)
 
 
 def with_halo(block, sides, width, periodic):
@@ -191,7 +198,7 @@
             damped = lax.cond(
                 is_polar, lambda inner: smooth(inner, start_row), lambda inner: inner, sector
             )
-            return lax.all_to_all(damped, "lon", split_axis=1, concat_axis=2, tiled=True)
+            return trade_parts(damped, "lon", 1, 2)
 
         filtered = filter_sector(
             lax.all_to_all(flattened, "lon", split_axis=2, concat_axis=1, tiled=True)

time: 514 us -> 367 us (0.71)
  local copies, waits for them, and re-layouts: 226 us -> 104 us
  other arithmetic: 65.3 us -> 19 us
  blocking collectives: 98.4 us -> 120 us
    unnamed x22 -> x83, local copies, waits for them, and re-layouts: 96.9 us -> 20.9 us
    mul x3, other arithmetic: 25.4 us -> 0.46 us  [local(): fields_now = fields_now + time_step * filtered.reshape(fields_now.shape)]
    mul x3, local copies, waits for them, and re-layouts: 24.3 us -> 0.39 us  [local(): fields_now = fields_now + time_step * filtered.reshape(fields_now.shape)]
    all_to_all x3, blocking collectives: 57.8 us -> 78.7 us  [trade_parts(): pieces = lax.all_to_all(pieces, axis, split_axis=0, concat_axis=0)]
    cond x15 -> x12, local copies, waits for them, and re-layouts: 18.4 us -> 2.14 us  [the longest x3 16.2 us: filter_sector(): lax.cond(is_polar, lambda inner: smooth(inner, start_row), lambda inner:...]
    all_to_all x3 -> x0, other arithmetic: 11.6 us -> none  [filter_sector(): lax.all_to_all(damped, 'lon', split_axis=1, concat_axis=2, tiled=True)]
  transfers between devices with their start and end apart: 13 -> 13, of which waited for: 5 -> 6; matrix products, arithmetic and copies ran while one was open for 2% -> 1% of each run, Pallas kernels for 0% -> 0%
where the time goes in v1:
time: 367 us; the launch traced here: 360 us
  blocking collectives  120 us (33%)
  local copies, waits for them, and re-layouts  104 us (28%)
  matrix products  54.3 us (15%)
  starting transfers between devices  32.5 us (9%)
  waiting for transfers between devices  28.4 us (8%)
  other arithmetic  19 us (5%)
    all_to_all x3, blocking collectives, trade_parts(): pieces = lax.all_to_all(pieces, axis, split_axis=0, concat_axis=0)  78.7 us
    all_to_all x2, blocking collectives, local(): lax.all_to_all(flattened, 'lon', split_axis=2, concat_axis=1, tiled=True)  40.9 us
    unnamed x83, local copies, waits for them, and re-layouts  20.9 us
    mul x9, local copies, waits for them, and re-layouts, smooth(): spec_re.reshape(vectors, slab_rows, total) * factors  18.9 us
    all_to_all x7, local copies, waits for them, and re-layouts, local(): lax.all_to_all(flattened, 'lon', split_axis=2, concat_axis=1, tiled=True)  18.3 us
    ppermute x6, starting transfers between devices, with_halo(): lax.ppermute(lax.slice_in_dim(block, block.shape[dim] - width, None, axis...  16.5 us
    all_to_all x1, waiting for transfers between devices, local(): lax.all_to_all(flattened, 'lon', split_axis=2, concat_axis=1, tiled=True)  16.2 us
    reshape x6, local copies, waits for them, and re-layouts, forward_real(): grid = signal.reshape(vectors, outer, inner)  15.7 us
  transfers between devices with their start and end apart: 13, of which 6 were waited for; matrix products, arithmetic and copies ran while one was open for 1% of the time, Pallas kernels for 0%

profile of v1, /device:TPU:96, one launch (start us, length us, event | category | flops | bytes accessed | tf_op | source)
XLA Modules:
  0.0 359.9 jit_solution(7687619554726092583)
XLA Ops:
  1.0 5.3 %collective-permute-start = (f32[6,2,1,128]{3,1,2,0:T(2,128)S(1)}, f32[6,2,1,128]{3,1,2,0:T(2,128)S(1)}, u32[]{:S(2)}, u32[]{:S(2)}) collective-permute-start(f32[6,2,1,128]{3,1,2,0:T(2,128)S(1)} %bitcast.432), channel_id=1, source_target_pairs={{1,0},{2,1},{3,2},{4,3},{5,4},{6,5},{7,6},{8,7},{9,8},{10,9},{11,1... | collective-permute-start | bytes 18440 | tf_op jit(solution)/shard_map/ppermute | solution.py:29
  10.0 5.0 %collective-permute-start.3 = (f32[6,2,144,1]{2,3,1,0:T(1,128)S(1)}, f32[6,2,144,1]{2,3,1,0:T(1,128)S(1)}, u32[]{:S(2)}, u32[]{:S(2)}) collective-permute-start(f32[6,2,144,1]{2,3,1,0:T(1,128)S(1)} %get-tuple-element.470), channel_id=1, source_target_pairs={{0,16},{16,32},{32,48},{48,64},{64,80},{80,96},{96,112},{112,128},... | collective-permute-start | bytes 20744 | tf_op jit(solution)/shard_map/ppermute | solution.py:26
  21.6 3.9 %reshape.286 = f32[16,1,13824]{2,1,0:T(1,128)} reshape(f32[128,12,144]{2,1,0:T(8,128)} %bitcast.413) | data formatting | bytes 1769472
  25.4 4.7 %all-to-all-start = ((f32[16,1,13824]{2,1,0:T(1,128)}), f32[16,1,13824]{2,1,0:T(1,128)S(1)}, u32[]{:S(2)}, u32[]{:S(2)}) async-start(f32[16,1,13824]{2,1,0:T(1,128)} %reshape.286), calls=%async_computation | async-start | bytes 1769472 | tf_op jit(solution)/shard_map/all_to_all | solution.py:204
  30.2 16.2 %all-to-all-done = f32[16,1,13824]{2,1,0:T(1,128)S(1)} async-done(((f32[16,1,13824]{2,1,0:T(1,128)}), f32[16,1,13824]{2,1,0:T(1,128)S(1)}, u32[]{:S(2)}, u32[]{:S(2)}) %all-to-all-start) | async-done | bytes 884768 | tf_op jit(solution)/shard_map/all_to_all | solution.py:204
  52.1 3.7 %copy.189 = f32[12,16,144,8]{2,1,3,0:T(8,128)} copy(f32[12,16,144,8]{2,0,3,1:T(8,128)} %bitcast.414) | data formatting | bytes 1769472 | tf_op jit(solution)/shard_map/all_to_all | solution.py:204
  58.0 35.6 %conditional.3 = (f32[1,12,144,8]{2,3,1,0:T(8,128)S(1)}, f32[1,12,144,8]{2,3,1,0:T(8,128)S(1)}, f32[1,12,144,8]{2,3,1,0:T(8,128)S(1)}, f32[1,12,144,8]{2,3,1,0:T...) conditional(s32[]{:T(128)} %convert_element_type.252, ...), branch_computations={%region_0.0_spmd, %region_1.2_spmd} | conditional | flops 1533790208 | bytes 48321928 | solution.py:198
  59.3 2.9 mul.1036
  62.2 2.9 copy.144
  65.1 2.9 reshape.271
  93.9 26.2 %all_to_all.81 = f32[16,12,144,8]{2,3,1,0:T(8,128)S(1)} all-to-all(f32[16,12,144,8]{2,3,1,0:T(8,128)S(1)} %constant_dynamic-update-slice_fusion), channel_id=1, replica_groups=mesh['lat'=16,'lon'=16] {'lon'}, dimensions={0} | all-to-all | bytes 1769472 | tf_op jit(solution)/shard_map/all_to_all | solution.py:15
  122.6 5.1 %collective-permute-start.7 = (f32[6,2,144,1]{2,3,1,0:T(1,128)S(1)}, f32[6,2,144,1]{2,3,1,0:T(1,128)S(1)}, u32[]{:S(2)}, u32[]{:S(2)}) collective-permute-start(f32[6,2,144,1]{2,3,1,0:T(1,128)S(1)} %get-tuple-element.468), channel_id=1, source_target_pairs={{0,16},{16,32},{32,48},{48,64},{64,80},{80,96},{96,112},{112,128},... | collective-permute-start | bytes 20744 | tf_op jit(solution)/shard_map/ppermute | solution.py:26
  130.0 5.3 %collective-permute-done.5 = f32[6,2,1,128]{3,1,2,0:T(2,128)S(1)} collective-permute-done((f32[6,2,1,128]{3,1,2,0:T(2,128)S(1)}, f32[6,2,1,128]{3,1,2,0:T(2,128)S(1)}, u32[]{:S(2)}, u32[]{:S(2)}) %collective-permute-start.5) | collective-permute-done | bytes 6176 | tf_op jit(solution)/shard_map/ppermute | solution.py:26
  140.9 3.2 reshape.288
  144.0 20.4 %all_to_all.82 = f32[16,1,13824]{2,1,0:T(1,128)} all-to-all(f32[16,1,13824]{2,1,0:T(1,128)S(1)} %reshape.288), channel_id=1, replica_groups=mesh['lat'=16,'lon'=16] {'lon'}, dimensions={0} | all-to-all | bytes 1769472 | tf_op jit(solution)/shard_map/all_to_all | solution.py:204
  164.5 3.8 %reduce.1 = f32[16,13824]{1,0:T(8,128)S(1)} reduce(f32[16,1,13824]{2,1,0:T(1,128)} %all_to_all.82, f32[]{:T(128)} %broadcast.839), dimensions={1}, to_apply=%all_to_all.65.reduce_sub_computation | reduce | bytes 1769476 | tf_op jit(solution)/shard_map/all_to_all | solution.py:204
  170.8 3.7 %copy.198 = f32[12,16,144,8]{2,1,3,0:T(8,128)} copy(f32[12,16,144,8]{2,0,3,1:T(8,128)} %bitcast.416) | data formatting | bytes 1769472 | tf_op jit(solution)/shard_map/all_to_all | solution.py:204
  176.7 37.1 %conditional.4 = (f32[1,12,144,8]{2,3,1,0:T(8,128)S(1)}, f32[1,12,144,8]{2,3,1,0:T(8,128)S(1)}, f32[1,12,144,8]{2,3,1,0:T(8,128)S(1)}, f32[1,12,144,8]{2,3,1,0:T...) conditional(s32[]{:T(128)} %convert_element_type.252, ...), branch_computations={%region_2.3_spmd, %region_3.4_spmd} | conditional | flops 1533790208 | bytes 48321928 | solution.py:198
  178.9 3.5 mul.1141
  182.4 2.9 copy.155
  185.3 2.9 reshape.272
  214.1 26.2 %all_to_all.83 = f32[16,12,144,8]{2,3,1,0:T(8,128)S(1)} all-to-all(f32[16,12,144,8]{2,3,1,0:T(8,128)S(1)} %constant_dynamic-update-slice_fusion.16), channel_id=1, replica_groups=mesh['lat'=16,'lon'=16] {'lon'}, dimensions={0} | all-to-all | bytes 1769472 | tf_op jit(solution)/shard_map/all_to_all | solution.py:15
  242.8 5.1 %collective-permute-start.11 = (f32[6,2,144,1]{2,3,1,0:T(1,128)S(1)}, f32[6,2,144,1]{2,3,1,0:T(1,128)S(1)}, u32[]{:S(2)}, u32[]{:S(2)}) collective-permute-start(f32[6,2,144,1]{2,3,1,0:T(1,128)S(1)} %get-tuple-element.464), channel_id=1, source_target_pairs={{0,16},{16,32},{32,48},{48,64},{64,80},{80,96},{96,112},{112,128},... | collective-permute-start | bytes 20744 | tf_op jit(solution)/shard_map/ppermute | solution.py:26
  250.2 5.3 %collective-permute-done.9 = f32[6,2,1,128]{3,1,2,0:T(2,128)S(1)} collective-permute-done((f32[6,2,1,128]{3,1,2,0:T(2,128)S(1)}, f32[6,2,1,128]{3,1,2,0:T(2,128)S(1)}, u32[]{:S(2)}, u32[]{:S(2)}) %collective-permute-start.9) | collective-permute-done | bytes 6176 | tf_op jit(solution)/shard_map/ppermute | solution.py:26
  261.0 3.2 reshape.290
  264.2 20.5 %all_to_all.84 = f32[16,1,13824]{2,1,0:T(1,128)S(1)} all-to-all(f32[16,1,13824]{2,1,0:T(1,128)S(1)} %reshape.290), channel_id=1, replica_groups=mesh['lat'=16,'lon'=16] {'lon'}, dimensions={0} | all-to-all | bytes 1769472 | tf_op jit(solution)/shard_map/all_to_all | solution.py:204
  289.9 3.7 %copy.206 = f32[12,16,144,8]{2,1,3,0:T(8,128)} copy(f32[12,16,144,8]{2,0,3,1:T(8,128)} %bitcast.418) | data formatting | bytes 1769472 | tf_op jit(solution)/shard_map/all_to_all | solution.py:204
  295.8 35.4 %conditional.5 = (f32[1,12,144,8]{2,3,1,0:T(8,128)S(1)}, f32[1,12,144,8]{2,3,1,0:T(8,128)S(1)}, f32[1,12,144,8]{2,3,1,0:T(8,128)S(1)}, f32[1,12,144,8]{2,3,1,0:T...) conditional(s32[]{:T(128)} %convert_element_type.252, ...), branch_computations={%region_4.5_spmd, %region_5.6_spmd} | conditional | flops 1533790208 | bytes 48321928 | solution.py:198
  297.1 2.9 mul.1246
  300.0 2.9 copy.166
  302.8 2.9 reshape.273
  331.5 26.2 %all_to_all.85 = f32[16,12,144,8]{2,3,1,0:T(8,128)S(1)} all-to-all(f32[16,12,144,8]{2,3,1,0:T(8,128)S(1)} %constant_dynamic-update-slice_fusion.32), channel_id=1, replica_groups=mesh['lat'=16,'lon'=16] {'lon'}, dimensions={0} | all-to-all | bytes 1769472 | tf_op jit(solution)/shard_map/all_to_all | solution.py:15
  (236 shorter events, 134.2 us)
Async XLA Ops:
  0.0 15.2 %copy-start.17 = (f32[2,128]{1,0:T(2,128)S(1)}, f32[2,128]{1,0:T(2,128)}, u32[]{:S(2)}) copy-start(f32[2,128]{1,0:T(2,128)} %param.13) | copy-start | bytes 3076
  0.0 15.2 %copy-start.16 = (f32[3,2]{0,1:T(2,128)S(1)}, f32[3,2]{0,1:T(2,128)}, u32[]{:S(2)}) copy-start(f32[3,2]{0,1:T(2,128)} %param.15) | copy-start | bytes 76
  0.9 14.8 %collective-permute-start.1 = (f32[6,2,1,128]{3,1,2,0:T(2,128)S(1)}, f32[6,2,1,128]{3,1,2,0:T(2,128)S(1)}, u32[]{:S(2)}, u32[]{:S(2)}) collective-permute-start(f32[6,2,1,128]{3,1,2,0:T(2,128)S(1)} %bitcast.431), channel_id=1, source_target_pairs={{0,1},{1,2},{2,3},{3,4},{4,5},{5,6},{6,7},{7,8},{8,9},{9,10},{10,1... | collective-permute-start | bytes 18440 | tf_op jit(solution)/shard_map/ppermute | solution.py:26
  1.0 15.5 %copy-start.3 = (f32[2,128]{1,0:T(2,128)S(1)}, f32[2,128]{1,0:T(2,128)}, u32[]{:S(2)}) copy-start(f32[2,128]{1,0:T(2,128)} %param.12) | copy-start | bytes 3076
  1.0 14.4 %collective-permute-start = (f32[6,2,1,128]{3,1,2,0:T(2,128)S(1)}, f32[6,2,1,128]{3,1,2,0:T(2,128)S(1)}, u32[]{:S(2)}, u32[]{:S(2)}) collective-permute-start(f32[6,2,1,128]{3,1,2,0:T(2,128)S(1)} %bitcast.432), channel_id=1, source_target_pairs={{1,0},{2,1},{3,2},{4,3},{5,4},{6,5},{7,6},{8,7},{9,8},{10,9},{11,1... | collective-permute-start | bytes 18440 | tf_op jit(solution)/shard_map/ppermute | solution.py:29
  8.0 8.0 %collective-permute-start.2 = (f32[6,2,144,1]{2,3,1,0:T(1,128)S(1)}, f32[6,2,144,1]{2,3,1,0:T(1,128)S(1)}, u32[]{:S(2)}, u32[]{:S(2)}) collective-permute-start(f32[6,2,144,1]{2,3,1,0:T(1,128)S(1)} %get-tuple-element.469), channel_id=1, source_target_pairs={{16,0},{32,16},{48,32},{64,48},{80,64},{96,80},{112,96},{128,112},... | collective-permute-start | bytes 20744 | tf_op jit(solution)/shard_map/ppermute | solution.py:29
  10.0 6.4 %collective-permute-start.3 = (f32[6,2,144,1]{2,3,1,0:T(1,128)S(1)}, f32[6,2,144,1]{2,3,1,0:T(1,128)S(1)}, u32[]{:S(2)}, u32[]{:S(2)}) collective-permute-start(f32[6,2,144,1]{2,3,1,0:T(1,128)S(1)} %get-tuple-element.470), channel_id=1, source_target_pairs={{0,16},{16,32},{32,48},{48,64},{64,80},{80,96},{96,112},{112,128},... | collective-permute-start | bytes 20744 | tf_op jit(solution)/shard_map/ppermute | solution.py:26
  15.2 3.3 copy-start.7
  15.2 3.3 copy-start.10
  15.3 3.2 copy-start.13
  18.2 0.7 copy-start.4
  25.4 21.0 %all-to-all-start = ((f32[16,1,13824]{2,1,0:T(1,128)}), f32[16,1,13824]{2,1,0:T(1,128)S(1)}, u32[]{:S(2)}, u32[]{:S(2)}) async-start(f32[16,1,13824]{2,1,0:T(1,128)} %reshape.286), calls=%async_computation | async-start | bytes 1769472 | tf_op jit(solution)/shard_map/all_to_all | solution.py:204
  73.3 1.5 copy-start
  120.7 15.0 %collective-permute-start.6 = (f32[6,2,144,1]{2,3,1,0:T(1,128)S(1)}, f32[6,2,144,1]{2,3,1,0:T(1,128)S(1)}, u32[]{:S(2)}, u32[]{:S(2)}) collective-permute-start(f32[6,2,144,1]{2,3,1,0:T(1,128)S(1)} %get-tuple-element.467), channel_id=1, source_target_pairs={{16,0},{32,16},{48,32},{64,48},{80,64},{96,80},{112,96},{128,112},... | collective-permute-start | bytes 20744 | tf_op jit(solution)/shard_map/ppermute | solution.py:29
  122.6 13.0 %collective-permute-start.7 = (f32[6,2,144,1]{2,3,1,0:T(1,128)S(1)}, f32[6,2,144,1]{2,3,1,0:T(1,128)S(1)}, u32[]{:S(2)}, u32[]{:S(2)}) collective-permute-start(f32[6,2,144,1]{2,3,1,0:T(1,128)S(1)} %get-tuple-element.468), channel_id=1, source_target_pairs={{0,16},{16,32},{32,48},{48,64},{64,80},{80,96},{96,112},{112,128},... | collective-permute-start | bytes 20744 | tf_op jit(solution)/shard_map/ppermute | solution.py:26
  128.3 1.4 collective-permute-start.4
  128.6 6.7 %collective-permute-start.5 = (f32[6,2,1,128]{3,1,2,0:T(2,128)S(1)}, f32[6,2,1,128]{3,1,2,0:T(2,128)S(1)}, u32[]{:S(2)}, u32[]{:S(2)}) collective-permute-start(f32[6,2,1,128]{3,1,2,0:T(2,128)S(1)} %copy.194), channel_id=1, source_target_pairs={{0,1},{1,2},{2,3},{3,4},{4,5},{5,6},{6,7},{7,8},{8,9},{9,10},{10,1... | collective-permute-start | bytes 18440 | tf_op jit(solution)/shard_map/ppermute | solution.py:26
  137.4 0.7 copy-start.5
  137.4 0.6 copy-start.8
  137.4 0.7 copy-start.11
  137.5 0.7 copy-start.14
  193.6 1.5 copy-start.1
  240.9 15.0 %collective-permute-start.10 = (f32[6,2,144,1]{2,3,1,0:T(1,128)S(1)}, f32[6,2,144,1]{2,3,1,0:T(1,128)S(1)}, u32[]{:S(2)}, u32[]{:S(2)}) collective-permute-start(f32[6,2,144,1]{2,3,1,0:T(1,128)S(1)} %get-tuple-element.463), channel_id=1, source_target_pairs={{16,0},{32,16},{48,32},{64,48},{80,64},{96,80},{112,96},{128,112},... | collective-permute-start | bytes 20744 | tf_op jit(solution)/shard_map/ppermute | solution.py:29
  242.8 13.0 %collective-permute-start.11 = (f32[6,2,144,1]{2,3,1,0:T(1,128)S(1)}, f32[6,2,144,1]{2,3,1,0:T(1,128)S(1)}, u32[]{:S(2)}, u32[]{:S(2)}) collective-permute-start(f32[6,2,144,1]{2,3,1,0:T(1,128)S(1)} %get-tuple-element.464), channel_id=1, source_target_pairs={{0,16},{16,32},{32,48},{48,64},{64,80},{80,96},{96,112},{112,128},... | collective-permute-start | bytes 20744 | tf_op jit(solution)/shard_map/ppermute | solution.py:26
  248.5 1.4 collective-permute-start.8
  248.8 6.7 %collective-permute-start.9 = (f32[6,2,1,128]{3,1,2,0:T(2,128)S(1)}, f32[6,2,1,128]{3,1,2,0:T(2,128)S(1)}, u32[]{:S(2)}, u32[]{:S(2)}) collective-permute-start(f32[6,2,1,128]{3,1,2,0:T(2,128)S(1)} %copy.202), channel_id=1, source_target_pairs={{0,1},{1,2},{2,3},{3,4},{4,5},{5,6},{6,7},{7,8},{8,9},{9,10},{10,1... | collective-permute-start | bytes 18440 | tf_op jit(solution)/shard_map/ppermute | solution.py:26
  257.6 0.7 copy-start.6
  257.6 0.6 copy-start.9
  257.6 0.7 copy-start.12
  257.6 0.7 copy-start.15
  311.0 1.5 copy-start.2
